TPU v7x, 32 devices: a whole 2x2x4 slice. The times are simulated.
32 devices in a mesh: sub: 8 (over y, x, core), grp: 4 (over z).
Axes of the slice: x: 2, y: 2, z: 4, core: 2. Of those that a mesh axis runs over, the one named last changes fastest.
Arguments:
- gaps: float32 [4, 16, 96, 1024], P('grp', 'sub'), may hold values from -6 to 6
- dual_op: bfloat16 [4, 16, 1024, 1024], P('grp', 'sub'), may hold values from -1 to 2.5, as said below
- dirichlet: bfloat16 [4, 16, 1024, 1024], P('grp', 'sub'), may hold values from -1 to 2.5, as said below
- modes: float32 [4, 16, 6, 1024], P('grp', 'sub'), may hold values from -6 to 6
- coarse_op: float32 [4, 16, 6, 384], P('grp', 'sub'), may hold values from -0.0009765625 to 0.0009765625, as said below
- slot_map: int32 [4, 16, 1024], P('grp', 'sub'), may hold values from 0 to 1023, as said below
Outputs:
- multipliers: float32 [4, 16, 96, 1024], P('grp', 'sub')
- residual: float32 [4, 16, 96, 1024], P('grp', 'sub')
Inputs may be any that keep to these rules, and one draw needn't show every extreme that they name: `dual_op`: each subdomain's block is symmetric positive definite. `dirichlet`: each subdomain's block is symmetric positive definite. The 384 x 384 matrix whose row (16 y + x) * 6 + k is coarse_op[y, x, k] is symmetric. `slot_map`: for every subdomain and face f, the entries f * 256 to (f + 1) * 256 - 1 are a permutation of those same slot numbers.
All inputs are finite; a program needn't handle non-finite values.
Results may differ from a plain program's by a relative error of at most 0.012.
The roundings to bfloat16 on the way count: a program that leaves them out, or rounds other values in their place, can miss the bound.
Values sent between devices are 32-bit elements; how exact they have to be, the bound alone decides.
No kernel may reach another device: no remote copies, remote signals or barrier semaphores. Data moves between devices by JAX's collectives and lax.ppermute only.
A program may use at most 128 MiB of HBM per device.

v0:
```python
import jax
import jax.numpy as jnp
from jax import lax
from jax.sharding import PartitionSpec as P

MODES = 6
ITERS = 2
HIGHEST = lax.Precision.HIGHEST


def extended(block, sides, width):
    for axis, dim in sides:
        count = lax.axis_size(axis)
        forward = [(i, i + 1) for i in range(count - 1)]
        backward = [(target, source) for source, target in forward]
        low = lax.ppermute(
            lax.slice_in_dim(block, block.shape[dim] - width, None, axis=dim), axis, forward
        )
        high = lax.ppermute(lax.slice_in_dim(block, 0, width, axis=dim), axis, backward)
        block = jnp.concatenate([low, block, high], axis=dim)
    return block


def inverse_map(maps):
    width = maps.shape[-1]

    def invert(perm_row):
        return jnp.zeros_like(perm_row).at[perm_row].set(jnp.arange(width, dtype=jnp.int32))

    return jax.vmap(invert)(maps)


def reorder_block(matrix, order):
    rows_first = jnp.take(matrix, order, axis=0)
    swapped = jnp.swapaxes(rows_first, 0, 1)
    both = jnp.take(swapped, order, axis=0)
    return jnp.swapaxes(both, 0, 1)


def jump_local(values):
    subdomains, columns, width = values.shape
    faces = values.reshape(subdomains, columns, 4, width // 4)
    edges = jnp.stack([faces[0, :, 0], faces[-1, :, 1]])
    beside = extended(edges, (("sub", 0),), 1)
    rims = jnp.stack([faces[:, :, 2], faces[:, :, 3]])
    across = extended(rims, (("grp", 0),), 1)
    from_left = jnp.concatenate([beside[0][None], faces[:-1, :, 1]], axis=0)
    from_right = jnp.concatenate([faces[1:, :, 0], beside[3][None]], axis=0)
    partner = jnp.stack([from_left, from_right, across[0], across[3]], axis=2)
    return (faces - partner).reshape(subdomains, columns, width)


def apply_blocks(values, matrices):
    return jnp.einsum(
        "snm,smk->snk", values.astype(jnp.bfloat16), matrices, preferred_element_type=jnp.float32
    )


def shards(gaps, dual_op, dirichlet, modes, coarse_op, slot_map):
    maps = slot_map[0]
    back_map = inverse_map(maps)
    vectors = jnp.take_along_axis(gaps[0], maps[:, None, :], axis=2)
    subdomains, columns, width = vectors.shape
    quarter = width // 4
    sub_total = lax.axis_size("sub")
    grp_total = lax.axis_size("grp")
    x_position = lax.axis_index("sub") * subdomains + jnp.arange(subdomains, dtype=jnp.int32)
    grp_here = lax.axis_index("grp")
    filler = jnp.ones((subdomains,), jnp.float32)
    face_weight = jnp.stack(
        [
            jnp.where(x_position == 0, 1.0, 2.0) * filler,
            jnp.where(x_position == sub_total * subdomains - 1, 1.0, 2.0) * filler,
            jnp.where(grp_here == 0, 1.0, 2.0) * filler,
            jnp.where(grp_here == grp_total - 1, 1.0, 2.0) * filler,
        ],
        axis=1,
    )
    slot_weight = jnp.repeat(face_weight, quarter, axis=1)
    ordered_modes = jnp.take_along_axis(modes[0], maps[:, None, :], axis=2)
    weighted_modes = ordered_modes * slot_weight[:, None, :]
    stiffness = jax.vmap(reorder_block)(dual_op[0], maps)
    schur_blocks = jax.vmap(reorder_block)(dirichlet[0], maps)
    rows_here = coarse_op[0].reshape(subdomains * MODES, -1)
    rows_count = rows_here.shape[0]
    rows_sub_major = rows_here.reshape(rows_count, grp_total, sub_total, rows_count)
    rows_sub_major = rows_sub_major.transpose(0, 2, 1, 3).reshape(rows_count, -1)
    coarse_total = rows_here.shape[1]
    face_modes = ordered_modes.reshape(subdomains, MODES, 4, quarter).transpose(0, 2, 1, 3)
    own_rows = rows_here.reshape(subdomains, 1, MODES, coarse_total)
    packed = jnp.concatenate(
        [face_modes, jnp.broadcast_to(own_rows, (subdomains, 4, MODES, coarse_total))], axis=3
    )
    edge_pack = jnp.stack([packed[0, 0], packed[-1, 1]])
    beside_pack = extended(edge_pack, (("sub", 0),), 1)
    rim_pack = jnp.stack([packed[:, 2], packed[:, 3]])
    across_pack = extended(rim_pack, (("grp", 0),), 1)
    left_pack = jnp.concatenate([beside_pack[0][None], packed[:-1, 1]], axis=0)
    right_pack = jnp.concatenate([packed[1:, 0], beside_pack[3][None]], axis=0)
    partner_pack = jnp.stack([left_pack, right_pack, across_pack[0], across_pack[3]], axis=1)
    partner_modes = partner_pack[:, :, :, :quarter]
    partner_rows = partner_pack[:, :, :, quarter:]

    def coefficients(values):
        return jnp.einsum("skm,snm->skn", weighted_modes, values, precision=HIGHEST)

    def gathered(coeffs):
        grouped = lax.all_gather(coeffs[None], "grp", axis=0, tiled=True)
        everything = lax.all_gather(grouped, "sub", axis=1, tiled=True)
        return everything.reshape(-1, columns)

    def amounts_of(flat):
        return jnp.dot(rows_here, flat, precision=HIGHEST, preferred_element_type=jnp.float32)

    def lift(amounts, flat):
        shaped = amounts.reshape(subdomains, MODES, columns)
        own_face = jnp.einsum("sfkm,skn->snfm", face_modes, shaped, precision=HIGHEST)
        far_amounts = jnp.einsum("sfkc,cn->sfkn", partner_rows, flat, precision=HIGHEST)
        far_face = jnp.einsum("sfkm,sfkn->snfm", partner_modes, far_amounts, precision=HIGHEST)
        return (own_face - far_face).reshape(subdomains, columns, width)

    def project(values):
        flat = gathered(coefficients(values))
        return values - lift(amounts_of(flat), flat)

    dual = jump_local(vectors)
    multipliers = jnp.zeros_like(dual)
    residual = project(dual)
    direction = jnp.zeros_like(dual)
    rho_prev = jnp.ones((columns,), jnp.float32)
    for step_index in range(ITERS):
        projected = project(residual)
        precond = jump_local(apply_blocks(projected, schur_blocks))
        rho_now = lax.psum(jnp.sum(projected * precond, axis=(0, 2)), ("sub", "grp"))
        search = project(precond)
        if step_index > 0:
            search = search + (rho_now / rho_prev)[None, :, None] * direction
        direction = search
        image = jump_local(apply_blocks(direction, stiffness))
        partial_dot = jnp.sum(direction * image, axis=(0, 2))
        curvature = lax.psum(partial_dot, ("sub", "grp"))
        step_len = rho_now / curvature
        multipliers = multipliers + step_len[None, :, None] * direction
        residual = residual - step_len[None, :, None] * image
        rho_prev = rho_now
    multipliers = jnp.take_along_axis(multipliers, back_map[:, None, :], axis=2)
    residual = jnp.take_along_axis(residual, back_map[:, None, :], axis=2)
    return (multipliers[None], residual[None])


def solution(mesh):
    placed = (
        P("grp", "sub", None, None),
        P("grp", "sub", None, None),
        P("grp", "sub", None, None),
        P("grp", "sub", None, None),
        P("grp", "sub", None, None),
        P("grp", "sub", None),
    )
    return jax.shard_map(
        shards,
        mesh=mesh,
        in_specs=placed,
        out_specs=(P("grp", "sub", None, None), P("grp", "sub", None, None)),
        check_vma=False,
    )
```

profile of v0, /device:TPU:0, one launch (start us, length us, event | category | flops | bytes accessed | tf_op | source)
XLA Modules:
  0.0 632.0 jit_solution(5257530324860456469)
XLA Ops:
  2.6 13.0 %gather_fusion = f32[2048,6]{1,0:T(8,128)S(1)} fusion(f32[2,6,1024]{1,2,0:T(8,128)S(1)} %bitcast.393, s32[2048]{0:T(1024)S(1)} %get-tuple-element.61), kind=kCustom, calls=%fused_computation.7 | custom fusion | bytes 114688 | tf_op jit(solution)/shard_map/jit(take_along_axis)/gather | solution.py:80
  17.6 2.4 collective-permute-start.4
  21.3 4.3 collective-permute-start.6
  27.3 13.0 %gather_fusion.1 = f32[2048,96]{1,0:T(8,128)S(1)} fusion(f32[2,96,1024]{1,2,0:T(8,128)S(1)} %bitcast.378, s32[2048]{0:T(1024)S(1)} %bitcast.377), kind=kCustom, calls=%fused_computation.clone | custom fusion | bytes 1589248 | tf_op jit(solution)/shard_map/jit(take_along_axis)/gather | solution.py:62
  41.5 4.0 collective-permute-start
  46.2 42.2 %gather_fusion.2 = bf16[2048,1024]{1,0:T(8,128)(2,1)} fusion(bf16[2,1024,1024]{2,1,0:T(8,128)(2,1)} %bitcast.375, s32[2048]{0:T(1024)S(1)} %get-tuple-element.60), kind=kCustom, calls=%fused_computation.1.clone | custom fusion | bytes 8404992 | tf_op jit(solution)/shard_map/vmap(jit(_take))/gather | solution.py:34
  88.4 6.2 copy.139
  94.6 42.0 %gather_fusion.4 = bf16[2048,1024]{1,0:T(8,128)(2,1)} fusion(bf16[2,1024,1024]{2,1,0:T(8,128)(2,1)} %bitcast.376, s32[2048]{0:T(1024)S(1)} %get-tuple-element.60), kind=kCustom, calls=%fused_computation.5.clone | custom fusion | bytes 8404992 | tf_op jit(solution)/shard_map/vmap(jit(_take))/gather | solution.py:34
  136.6 6.3 copy.148
  143.1 8.0 %scatter_custom_fusion = s32[2048]{0:T(1024)S(1)} fusion(s32[2048]{0:T(1024)S(1)} %get-tuple-element.65, s32[2048]{0:T(1024)S(1)} %get-tuple-element.64, s32[]{:T(128)} %constant.29.clone.1), kind=kCustom, calls=%fused_computation.184 | custom fusion | bytes 8196
  151.3 7.5 %select_bitcast_fusion = (bf16[2,1024,1024]{2,1,0:T(8,128)(2,1)}, bf16[2,1024,1024]{2,1,0:T(8,128)(2,1)}) fusion(bf16[2,1024,1024]{1,2,0:T(8,128)(2,1)} %copy.148, pred[2,1024]{1,0:T(4,128)(4,1)S(1)} %compare_and_fusion.1, bf16[2,1024,1024]{1,2,0:T(8,128)(2,1)} %copy.139), kind=kLoop, calls=%fused_computation.9 | loop fusion | flops 4194304 | bytes 16779264 | tf_op jit(solution)/shard_map/vmap()/transpose | solution.py:35
  159.4 40.6 %gather_fusion.3 = bf16[2048,1024]{1,0:T(8,128)(2,1)} fusion(bf16[2,1024,1024]{2,1,0:T(8,128)(2,1)} %get-tuple-element.57, s32[2048]{0:T(1024)S(1)} %get-tuple-element.60), kind=kCustom, calls=%fused_computation.4.clone | custom fusion | bytes 8404992 | tf_op jit(solution)/shard_map/vmap(jit(_take))/gather | solution.py:36
  200.0 40.7 %gather_fusion.5 = bf16[2048,1024]{1,0:T(8,128)(2,1)} fusion(bf16[2,1024,1024]{2,1,0:T(8,128)(2,1)} %get-tuple-element.56, s32[2048]{0:T(1024)S(1)} %get-tuple-element.60), kind=kCustom, calls=%fused_computation.6.clone | custom fusion | bytes 8404992 | tf_op jit(solution)/shard_map/vmap(jit(_take))/gather | solution.py:36
  242.0 4.1 collective-permute-start.2
  249.3 4.6 collective-permute-done.3
  255.9 13.5 %all-gather = f32[8,6,96]{2,1,0:T(8,128)S(1)} all-gather(f32[2,6,96]{2,1,0:T(8,128)S(1)} %fusion.40), channel_id=2, replica_groups=mesh['sub'=8,'grp'=4] {'grp'}, dimensions={0}, use_global_device_ids=true | all-gather | bytes 23040 | tf_op jit(solution)/shard_map/all_gather | solution.py:108
  269.5 13.7 %all_gather.31 = f32[4,16,6,96]{3,2,1,0:T(8,128)S(1)} all-gather(f32[4,2,6,96]{3,2,1,0:T(8,128)S(1)} %bitcast.410), channel_id=1, replica_groups=mesh['sub'=8,'grp'=4] {'sub'}, dimensions={1}, use_global_device_ids=true | all-gather | bytes 165888 | tf_op jit(solution)/shard_map/all_gather | solution.py:109
  286.4 13.1 %all-gather.1 = f32[8,6,96]{2,1,0:T(8,128)S(1)} all-gather(f32[2,6,96]{2,1,0:T(8,128)S(1)} %fusion.38), channel_id=3, replica_groups=mesh['sub'=8,'grp'=4] {'grp'}, dimensions={0}, use_global_device_ids=true | all-gather | bytes 23040 | tf_op jit(solution)/shard_map/all_gather | solution.py:108
  299.5 7.9 %all_gather.33 = f32[4,16,6,96]{3,2,1,0:T(8,128)S(1)} all-gather(f32[4,2,6,96]{3,2,1,0:T(8,128)S(1)} %bitcast.411), channel_id=1, replica_groups=mesh['sub'=8,'grp'=4] {'sub'}, dimensions={1}, use_global_device_ids=true | all-gather | bytes 165888 | tf_op jit(solution)/shard_map/all_gather | solution.py:109
  310.2 1.7 fusion.1
  312.6 2.3 collective-permute-start.8
  321.8 4.7 collective-permute-done.11
  329.9 13.2 %all-gather.2 = f32[8,6,96]{2,1,0:T(8,128)S(1)} all-gather(f32[2,6,96]{2,1,0:T(8,128)S(1)} %fusion.36), channel_id=4, replica_groups=mesh['sub'=8,'grp'=4] {'grp'}, dimensions={0}, use_global_device_ids=true | all-gather | bytes 23040 | tf_op jit(solution)/shard_map/all_gather | solution.py:108
  343.0 11.7 %all_gather.35 = f32[4,16,6,96]{3,2,1,0:T(8,128)S(1)} all-gather(f32[4,2,6,96]{3,2,1,0:T(8,128)S(1)} %bitcast.412), channel_id=1, replica_groups=mesh['sub'=8,'grp'=4] {'sub'}, dimensions={1}, use_global_device_ids=true | all-gather | bytes 165888 | tf_op jit(solution)/shard_map/all_gather | solution.py:109
  357.5 1.8 fusion.3
  360.0 2.3 collective-permute-start.12
  367.6 3.0 collective-permute-done.14
  370.6 4.4 collective-permute-done.15
  378.7 39.3 %all-reduce = (f32[96]{0:T(128)S(1)}, f32[96]{0:T(128)S(1)}) all-reduce(f32[96]{0:T(128)S(1)} %get-tuple-element.12, f32[96]{0:T(128)S(1)} %get-tuple-element.10), channel_id=1, replica_groups=mesh['sub'=8,'grp'=4] {'sub','grp'}, use_global_device_ids=true, to_apply=%region_1.4 | all-reduce | flops 192 | bytes 1536 | tf_op jit(solution)/shard_map/psum | solution.py:134
  419.0 13.1 %all-gather.3 = f32[8,6,96]{2,1,0:T(8,128)S(1)} all-gather(f32[2,6,96]{2,1,0:T(8,128)S(1)} %fusion.34), channel_id=5, replica_groups=mesh['sub'=8,'grp'=4] {'grp'}, dimensions={0}, use_global_device_ids=true | all-gather | bytes 23040 | tf_op jit(solution)/shard_map/all_gather | solution.py:108
  432.1 10.5 %all_gather.37 = f32[4,16,6,96]{3,2,1,0:T(8,128)S(1)} all-gather(f32[4,2,6,96]{3,2,1,0:T(8,128)S(1)} %bitcast.413), channel_id=1, replica_groups=mesh['sub'=8,'grp'=4] {'sub'}, dimensions={1}, use_global_device_ids=true | all-gather | bytes 165888 | tf_op jit(solution)/shard_map/all_gather | solution.py:109
  445.9 1.8 fusion
  448.4 2.3 collective-permute-start.16
  453.6 4.6 collective-permute-start.18
  459.0 2.3 collective-permute-done.19
  461.3 1.8 collective-permute-done.18
  465.1 1.9 multiply_reduce_fusion.1
  467.7 13.2 %all-gather.4 = f32[8,6,96]{2,1,0:T(8,128)S(1)} all-gather(f32[2,6,96]{2,1,0:T(8,128)S(1)} %fusion.32), channel_id=6, replica_groups=mesh['sub'=8,'grp'=4] {'grp'}, dimensions={0}, use_global_device_ids=true | all-gather | bytes 23040 | tf_op jit(solution)/shard_map/all_gather | solution.py:108
  480.9 10.2 %all_gather.39 = f32[4,16,6,96]{3,2,1,0:T(8,128)S(1)} all-gather(f32[4,2,6,96]{3,2,1,0:T(8,128)S(1)} %bitcast.414), channel_id=1, replica_groups=mesh['sub'=8,'grp'=4] {'sub'}, dimensions={1}, use_global_device_ids=true | all-gather | bytes 165888 | tf_op jit(solution)/shard_map/all_gather | solution.py:109
  491.7 38.7 %psum.30 = f32[96]{0:T(128)S(1)} all-reduce(f32[96]{0:T(128)S(1)} %get-tuple-element.8), channel_id=1, replica_groups=mesh['sub'=8,'grp'=4] {'sub','grp'}, use_global_device_ids=true, to_apply=%region_5.8 | all-reduce | flops 96 | bytes 768 | tf_op jit(solution)/shard_map/psum | solution.py:134
  532.6 2.5 fusion.2
  539.8 3.4 collective-permute-start.22
  546.4 4.4 collective-permute-done.23
  552.8 2.5 multiply_reduce_fusion
  555.4 43.3 %psum.31 = f32[96]{0:T(128)S(1)} all-reduce(f32[96]{0:T(128)S(1)} %get-tuple-element.6), channel_id=1, replica_groups=mesh['sub'=8,'grp'=4] {'sub','grp'}, use_global_device_ids=true, to_apply=%region_7.10 | all-reduce | flops 96 | bytes 768 | tf_op jit(solution)/shard_map/psum | solution.py:141
  598.7 2.3 multiply_subtract_fusion
  602.5 13.0 %gather_fusion.6 = f32[2048,96]{1,0:T(8,128)S(1)} fusion(f32[2,96,1024]{1,2,0:T(8,128)S(1)} %copy.169, s32[2048]{0:T(1024)S(1)} %bitcast.373), kind=kCustom, calls=%fused_computation.2.clone | custom fusion | bytes 1589248 | tf_op jit(solution)/shard_map/jit(take_along_axis)/gather | solution.py:146
  617.1 13.0 %gather_fusion.7 = f32[2048,96]{1,0:T(8,128)S(1)} fusion(f32[2,96,1024]{1,2,0:T(8,128)S(1)} %copy.171, s32[2048]{0:T(1024)S(1)} %bitcast.374), kind=kCustom, calls=%fused_computation.3.clone | custom fusion | bytes 1589248 | tf_op jit(solution)/shard_map/jit(take_along_axis)/gather | solution.py:147
  (208 shorter events, 73.4 us)
Async XLA Ops:
  0.6 26.3 %copy-start.10 = (s32[1,2,1024]{2,1,0:T(2,128)S(1)}, s32[1,2,1024]{2,1,0:T(2,128)}, u32[]{:S(2)}) copy-start(s32[1,2,1024]{2,1,0:T(2,128)} %param.15) | copy-start | bytes 24580
  0.6 26.3 %copy-start.9 = (f32[1,2,96,1024]{3,2,1,0:T(8,128)S(1)}, f32[1,2,96,1024]{3,2,1,0:T(8,128)}, u32[]{:S(2)}) copy-start(f32[1,2,96,1024]{3,2,1,0:T(8,128)} %param.10) | copy-start | bytes 2359300
  17.6 223.1 %collective-permute-start.4 = (f32[1,6,640]{2,1,0:T(8,128)S(1)}, f32[1,6,640]{2,1,0:T(8,128)S(1)}, u32[]{:S(2)}, u32[]{:S(2)}) collective-permute-start(f32[1,6,640]{2,1,0:T(8,128)S(1)} %get-tuple-element.44), channel_id=1, source_target_pairs={{0,4},{4,8},{8,12},{12,16},{16,20},{20,24},{24,28},{1,5},{5,9},{9,... | collective-permute-start | bytes 46088 | tf_op jit(solution)/shard_map/ppermute | solution.py:16
  19.9 222.1 %collective-permute-start.5 = (f32[1,6,640]{2,1,0:T(8,128)S(1)}, f32[1,6,640]{2,1,0:T(8,128)S(1)}, u32[]{:S(2)}, u32[]{:S(2)}) collective-permute-start(f32[1,6,640]{2,1,0:T(8,128)S(1)} %get-tuple-element.45), channel_id=1, source_target_pairs={{4,0},{8,4},{12,8},{16,12},{20,16},{24,20},{28,24},{5,1},{9,5},{13... | collective-permute-start | bytes 46088 | tf_op jit(solution)/shard_map/ppermute | solution.py:19
  21.3 224.9 %collective-permute-start.6 = (f32[1,2,6,640]{3,2,1,0:T(8,128)S(1)}, f32[1,2,6,640]{3,2,1,0:T(8,128)S(1)}, u32[]{:S(2)}, u32[]{:S(2)}) collective-permute-start(f32[1,2,6,640]{3,2,1,0:T(8,128)S(1)} %get-tuple-element.48), channel_id=1, source_target_pairs={{0,1},{1,2},{2,3},{4,5},{5,6},{6,7},{8,9},{9,10},{10,11},{12,13},{... | collective-permute-start | bytes 92168 | tf_op jit(solution)/shard_map/ppermute | solution.py:16
  25.6 222.0 %collective-permute-start.7 = (f32[1,2,6,640]{3,2,1,0:T(8,128)S(1)}, f32[1,2,6,640]{3,2,1,0:T(8,128)S(1)}, u32[]{:S(2)}, u32[]{:S(2)}) collective-permute-start(f32[1,2,6,640]{3,2,1,0:T(8,128)S(1)} %get-tuple-element.49), channel_id=1, source_target_pairs={{1,0},{2,1},{3,2},{5,4},{6,5},{7,6},{9,8},{10,9},{11,10},{13,12},{... | collective-permute-start | bytes 92168 | tf_op jit(solution)/shard_map/ppermute | solution.py:19
  41.5 206.2 %collective-permute-start = (f32[1,96,256]{2,0,1:T(1,128)S(1)}, f32[1,96,256]{2,0,1:T(1,128)S(1)}, u32[]{:S(2)}, u32[]{:S(2)}) collective-permute-start(f32[1,96,256]{2,0,1:T(1,128)S(1)} %get-tuple-element.38), channel_id=1, source_target_pairs={{0,4},{4,8},{8,12},{12,16},{16,20},{20,24},{24,28},{1,5},{5,9},{9,... | collective-permute-start | bytes 294920 | tf_op jit(solution)/shard_map/ppermute | solution.py:16
  45.9 105.4 %copy-start.12 = (pred[2,1024]{1,0:T(4,128)(4,1)}, pred[2,1024]{1,0:T(4,128)(4,1)S(1)}, u32[]{:S(2)}) copy-start(pred[2,1024]{1,0:T(4,128)(4,1)S(1)} %compare_and_fusion.1) | copy-start | bytes 6148
  136.6 6.3 copy-start.15
  136.6 6.4 %copy-start.16 = (s32[2]{0:T(128)S(1)}, s32[2]{0:T(128)}, u32[]{:S(2)}) copy-start(s32[2]{0:T(128)} %constant.70) | copy-start | bytes 28
  151.3 8.1 %copy-start.11 = (f32[1,2,6,384]{3,1,2,0:T(2,128)S(1)}, f32[1,2,6,384]{3,1,2,0:T(2,128)}, u32[]{:S(2)}) copy-start(f32[1,2,6,384]{3,1,2,0:T(2,128)} %param.14) | copy-start | bytes 55300
  240.7 7.4 %collective-permute-start.1 = (f32[1,96,256]{2,0,1:T(1,128)S(1)}, f32[1,96,256]{2,0,1:T(1,128)S(1)}, u32[]{:S(2)}, u32[]{:S(2)}) collective-permute-start(f32[1,96,256]{2,0,1:T(1,128)S(1)} %get-tuple-element.39), channel_id=1, source_target_pairs={{4,0},{8,4},{12,8},{16,12},{20,16},{24,20},{28,24},{5,1},{9,5},{13... | collective-permute-start | bytes 294920 | tf_op jit(solution)/shard_map/ppermute | solution.py:19
  242.0 7.3 %collective-permute-start.2 = (f32[1,2,96,256]{3,0,2,1:T(1,128)S(1)}, f32[1,2,96,256]{3,0,2,1:T(1,128)S(1)}, u32[]{:S(2)}, u32[]{:S(2)}) collective-permute-start(f32[1,2,96,256]{3,0,2,1:T(1,128)S(1)} %get-tuple-element.42), channel_id=1, source_target_pairs={{0,1},{1,2},{2,3},{4,5},{5,6},{6,7},{8,9},{9,10},{10,11},{12,13},{... | collective-permute-start | bytes 589832 | tf_op jit(solution)/shard_map/ppermute | solution.py:16
  246.2 7.7 %collective-permute-start.3 = (f32[1,2,96,256]{3,0,2,1:T(1,128)S(1)}, f32[1,2,96,256]{3,0,2,1:T(1,128)S(1)}, u32[]{:S(2)}, u32[]{:S(2)}) collective-permute-start(f32[1,2,96,256]{3,0,2,1:T(1,128)S(1)} %get-tuple-element.43), channel_id=1, source_target_pairs={{1,0},{2,1},{3,2},{5,4},{6,5},{7,6},{9,8},{10,9},{11,10},{13,12},{... | collective-permute-start | bytes 589832 | tf_op jit(solution)/shard_map/ppermute | solution.py:19
  285.6 24.2 %copy-start.13 = (pred[2,1024]{1,0:T(4,128)(4,1)S(1)}, pred[2,1024]{1,0:T(4,128)(4,1)}, u32[]{:S(2)}) copy-start(pred[2,1024]{1,0:T(4,128)(4,1)} %copy-done.12) | copy-start | bytes 6148
  308.0 2.2 copy-start.2
  309.9 2.4 copy-start.8
  312.6 7.0 %collective-permute-start.8 = (f32[1,96,256]{2,0,1:T(1,128)S(1)}, f32[1,96,256]{2,0,1:T(1,128)S(1)}, u32[]{:S(2)}, u32[]{:S(2)}) collective-permute-start(f32[1,96,256]{2,0,1:T(1,128)S(1)} %get-tuple-element.32), channel_id=1, source_target_pairs={{0,4},{4,8},{8,12},{12,16},{16,20},{20,24},{24,28},{1,5},{5,9},{9,... | collective-permute-start | bytes 294920 | tf_op jit(solution)/shard_map/ppermute | solution.py:16
  315.2 4.8 collective-permute-start.9
  316.5 5.3 collective-permute-start.10
  318.1 8.5 %collective-permute-start.11 = (f32[1,2,96,256]{3,0,2,1:T(1,128)S(1)}, f32[1,2,96,256]{3,0,2,1:T(1,128)S(1)}, u32[]{:S(2)}, u32[]{:S(2)}) collective-permute-start(f32[1,2,96,256]{3,0,2,1:T(1,128)S(1)} %get-tuple-element.37), channel_id=1, source_target_pairs={{1,0},{2,1},{3,2},{5,4},{6,5},{7,6},{9,8},{10,9},{11,10},{13,12},{... | collective-permute-start | bytes 589832 | tf_op jit(solution)/shard_map/ppermute | solution.py:19
  355.3 2.2 copy-start
  359.3 16.5 %copy-start.6 = (f32[2,96,1024]{2,1,0:T(8,128)}, f32[2,96,1024]{2,1,0:T(8,128)S(1)}, u32[]{:S(2)}) copy-start(f32[2,96,1024]{2,1,0:T(8,128)S(1)} %fusion.3) | copy-start | bytes 2359300
  360.0 6.9 %collective-permute-start.12 = (f32[1,96,256]{2,0,1:T(1,128)S(1)}, f32[1,96,256]{2,0,1:T(1,128)S(1)}, u32[]{:S(2)}, u32[]{:S(2)}) collective-permute-start(f32[1,96,256]{2,0,1:T(1,128)S(1)} %get-tuple-element.26), channel_id=1, source_target_pairs={{0,4},{4,8},{8,12},{12,16},{16,20},{20,24},{24,28},{1,5},{5,9},{9,... | collective-permute-start | bytes 294920 | tf_op jit(solution)/shard_map/ppermute | solution.py:16
  362.6 4.7 collective-permute-start.13
  363.9 6.7 %collective-permute-start.14 = (f32[1,2,96,256]{3,0,2,1:T(1,128)S(1)}, f32[1,2,96,256]{3,0,2,1:T(1,128)S(1)}, u32[]{:S(2)}, u32[]{:S(2)}) collective-permute-start(f32[1,2,96,256]{3,0,2,1:T(1,128)S(1)} %get-tuple-element.30), channel_id=1, source_target_pairs={{0,1},{1,2},{2,3},{4,5},{5,6},{6,7},{8,9},{9,10},{10,11},{12,13},{... | collective-permute-start | bytes 589832 | tf_op jit(solution)/shard_map/ppermute | solution.py:16
  365.5 9.5 %collective-permute-start.15 = (f32[1,2,96,256]{3,0,2,1:T(1,128)S(1)}, f32[1,2,96,256]{3,0,2,1:T(1,128)S(1)}, u32[]{:S(2)}, u32[]{:S(2)}) collective-permute-start(f32[1,2,96,256]{3,0,2,1:T(1,128)S(1)} %get-tuple-element.31), channel_id=1, source_target_pairs={{1,0},{2,1},{3,2},{5,4},{6,5},{7,6},{9,8},{10,9},{11,10},{13,12},{... | collective-permute-start | bytes 589832 | tf_op jit(solution)/shard_map/ppermute | solution.py:19
  443.1 2.8 copy-start.3
  445.0 0.9 copy-start.7
  447.7 16.1 %copy-start.5 = (f32[2,96,1024]{2,1,0:T(8,128)}, f32[2,96,1024]{2,1,0:T(8,128)S(1)}, u32[]{:S(2)}) copy-start(f32[2,96,1024]{2,1,0:T(8,128)S(1)} %fusion) | copy-start | bytes 2359300
  448.4 9.8 %collective-permute-start.16 = (f32[1,96,256]{2,0,1:T(1,128)S(1)}, f32[1,96,256]{2,0,1:T(1,128)S(1)}, u32[]{:S(2)}, u32[]{:S(2)}) collective-permute-start(f32[1,96,256]{2,0,1:T(1,128)S(1)} %get-tuple-element.20), channel_id=1, source_target_pairs={{0,4},{4,8},{8,12},{12,16},{16,20},{20,24},{24,28},{1,5},{5,9},{9,... | collective-permute-start | bytes 294920 | tf_op jit(solution)/shard_map/ppermute | solution.py:16
  451.0 7.6 %collective-permute-start.17 = (f32[1,96,256]{2,0,1:T(1,128)S(1)}, f32[1,96,256]{2,0,1:T(1,128)S(1)}, u32[]{:S(2)}, u32[]{:S(2)}) collective-permute-start(f32[1,96,256]{2,0,1:T(1,128)S(1)} %get-tuple-element.21), channel_id=1, source_target_pairs={{4,0},{8,4},{12,8},{16,12},{20,16},{24,20},{28,24},{5,1},{9,5},{13... | collective-permute-start | bytes 294920 | tf_op jit(solution)/shard_map/ppermute | solution.py:19
  452.3 9.0 %collective-permute-start.19 = (f32[1,2,96,256]{3,0,2,1:T(1,128)S(1)}, f32[1,2,96,256]{3,0,2,1:T(1,128)S(1)}, u32[]{:S(2)}, u32[]{:S(2)}) collective-permute-start(f32[1,2,96,256]{3,0,2,1:T(1,128)S(1)} %get-tuple-element.25), channel_id=1, source_target_pairs={{1,0},{2,1},{3,2},{5,4},{6,5},{7,6},{9,8},{10,9},{11,10},{13,12},{... | collective-permute-start | bytes 589832 | tf_op jit(solution)/shard_map/ppermute | solution.py:19
  453.6 9.5 %collective-permute-start.18 = (f32[1,2,96,256]{3,0,2,1:T(1,128)S(1)}, f32[1,2,96,256]{3,0,2,1:T(1,128)S(1)}, u32[]{:S(2)}, u32[]{:S(2)}) collective-permute-start(f32[1,2,96,256]{3,0,2,1:T(1,128)S(1)} %get-tuple-element.24), channel_id=1, source_target_pairs={{0,1},{1,2},{2,3},{4,5},{5,6},{6,7},{8,9},{9,10},{10,11},{12,13},{... | collective-permute-start | bytes 589832 | tf_op jit(solution)/shard_map/ppermute | solution.py:16
  530.4 2.2 copy-start.1
  536.9 7.7 %collective-permute-start.20 = (f32[1,96,256]{2,0,1:T(1,128)S(1)}, f32[1,96,256]{2,0,1:T(1,128)S(1)}, u32[]{:S(2)}, u32[]{:S(2)}) collective-permute-start(f32[1,96,256]{2,0,1:T(1,128)S(1)} %get-tuple-element.14), channel_id=1, source_target_pairs={{0,4},{4,8},{8,12},{12,16},{16,20},{20,24},{24,28},{1,5},{5,9},{9,... | collective-permute-start | bytes 294920 | tf_op jit(solution)/shard_map/ppermute | solution.py:16
  538.5 6.5 %collective-permute-start.21 = (f32[1,96,256]{2,0,1:T(1,128)S(1)}, f32[1,96,256]{2,0,1:T(1,128)S(1)}, u32[]{:S(2)}, u32[]{:S(2)}) collective-permute-start(f32[1,96,256]{2,0,1:T(1,128)S(1)} %get-tuple-element.15), channel_id=1, source_target_pairs={{4,0},{8,4},{12,8},{16,12},{20,16},{24,20},{28,24},{5,1},{9,5},{13... | collective-permute-start | bytes 294920 | tf_op jit(solution)/shard_map/ppermute | solution.py:19
  539.8 6.6 %collective-permute-start.22 = (f32[1,2,96,256]{3,0,2,1:T(1,128)S(1)}, f32[1,2,96,256]{3,0,2,1:T(1,128)S(1)}, u32[]{:S(2)}, u32[]{:S(2)}) collective-permute-start(f32[1,2,96,256]{3,0,2,1:T(1,128)S(1)} %get-tuple-element.18), channel_id=1, source_target_pairs={{0,1},{1,2},{2,3},{4,5},{5,6},{6,7},{8,9},{9,10},{10,11},{12,13},{... | collective-permute-start | bytes 589832 | tf_op jit(solution)/shard_map/ppermute | solution.py:16
  543.3 7.6 %collective-permute-start.23 = (f32[1,2,96,256]{3,0,2,1:T(1,128)S(1)}, f32[1,2,96,256]{3,0,2,1:T(1,128)S(1)}, u32[]{:S(2)}, u32[]{:S(2)}) collective-permute-start(f32[1,2,96,256]{3,0,2,1:T(1,128)S(1)} %get-tuple-element.19), channel_id=1, source_target_pairs={{1,0},{2,1},{3,2},{5,4},{6,5},{7,6},{9,8},{10,9},{11,10},{13,12},{... | collective-permute-start | bytes 589832 | tf_op jit(solution)/shard_map/ppermute | solution.py:19
  617.1 13.4 %copy-start.4 = (f32[2,1024,96]{1,2,0:T(8,128)S(1)}, f32[2,1024,96]{1,2,0:T(8,128)}, u32[]{:S(2)}) copy-start(f32[2,1024,96]{1,2,0:T(8,128)} %copy.170) | copy-start | bytes 2359300
  617.1 13.4 %copy-start.14 = (pred[2,1024]{1,0:T(4,128)(4,1)S(1)}, pred[2,1024]{1,0:T(4,128)(4,1)}, u32[]{:S(2)}) copy-start(pred[2,1024]{1,0:T(4,128)(4,1)} %and_bitcast_fusion) | copy-start | bytes 6148
where the time goes:
time: 644 us; the launch traced here: 632 us
  local copies, waits for them, and re-layouts  260 us (40%)
  blocking collectives  241 us (37%)
  starting transfers between devices  49.9 us (8%)
  waiting for transfers between devices  28.5 us (4%)
  other arithmetic  27.6 us (4%)
  matrix products  22.5 us (3%)
    gather x5, local copies, waits for them, and re-layouts, reorder_block(): rows_first = jnp.take(matrix, order, axis=0)  96.7 us
    gather x2, local copies, waits for them, and re-layouts, reorder_block(): both = jnp.take(swapped, order, axis=0)  81.3 us
    psum x2, blocking collectives, shards(): lax.psum(jnp.sum(projected * precond, axis=(0, 2)), ('sub', 'grp'))  78 us
    all_gather x5, blocking collectives, gathered(): grouped = lax.all_gather(coeffs[None], 'grp', axis=0, tiled=True)  66.2 us
    all_gather x5, blocking collectives, gathered(): everything = lax.all_gather(grouped, 'sub', axis=1, tiled=True)  53.9 us
    psum x1, blocking collectives, shards(): curvature = lax.psum(partial_dot, ('sub', 'grp'))  43.3 us
    ppermute x12, starting transfers between devices, extended(): lax.ppermute(lax.slice_in_dim(block, block.shape[dim] - width, None, axis...  34 us
    ppermute x12, waiting for transfers between devices, extended(): lax.ppermute(lax.slice_in_dim(block, 0, width, axis=dim), axis, backward)  20.5 us
  transfers between devices with their start and end apart: 24, of which 10 were waited for; matrix products, arithmetic and copies ran while one was open for 34% of the time, Pallas kernels for 0%

commit v1 on v0

--- a/solution.py
+++ b/solution.py
@@ -105,7 +105,15 @@
         return jnp.einsum("skm,snm->skn", weighted_modes, values, precision=HIGHEST)
 
     def gathered(coeffs):
-        grouped = lax.all_gather(coeffs[None], "grp", axis=0, tiled=True)
+        ways, here, step = (lax.axis_size("grp"), lax.axis_index("grp"), coeffs[None].shape[0])
+        line, have = (coeffs[None], 1)
+        while have < ways:
+            line = jnp.concatenate(
+                [line, lax.ppermute(line, "grp", [(d, (d - have) % ways) for d in range(ways)])],
+                axis=0,
+            )
+            have = 2 * have
+        grouped = jnp.roll(line, here * step, axis=0)
         everything = lax.all_gather(grouped, "sub", axis=1, tiled=True)
         return everything.reshape(-1, columns)
 

time: 644 us -> 621 us (0.964)
  blocking collectives: 241 us -> 173 us
  starting transfers between devices: 49.9 us -> 72.4 us
  waiting for transfers between devices: 28.5 us -> 45.4 us
    all_gather x5 -> x0, blocking collectives: 66.2 us -> none  [gathered(): grouped = lax.all_gather(coeffs[None], 'grp', axis=0, tiled=True)]
    ppermute x0 -> x10, starting transfers between devices: none -> 19.3 us  [gathered(): lax.ppermute(line, 'grp', [(d, (d - have) % ways) for d in range(ways)])]
    ppermute x0 -> x10, waiting for transfers between devices: none -> 14 us  [gathered(): lax.ppermute(line, 'grp', [(d, (d - have) % ways) for d in range(ways)])]
  transfers between devices with their start and end apart: 24 -> 34, of which waited for: 10 -> 15; matrix products, arithmetic and copies ran while one was open for 34% -> 35% of each run, Pallas kernels for 0% -> 0%
where the time goes in v1:
time: 621 us; the launch traced here: 610 us
  local copies, waits for them, and re-layouts  261 us (42%)
  blocking collectives  173 us (28%)
  starting transfers between devices  72.4 us (12%)
  waiting for transfers between devices  45.4 us (7%)
  other arithmetic  34 us (5%)
  matrix products  22.4 us (4%)
    gather x5, local copies, waits for them, and re-layouts, reorder_block(): rows_first = jnp.take(matrix, order, axis=0)  96.7 us
    gather x2, local copies, waits for them, and re-layouts, reorder_block(): both = jnp.take(swapped, order, axis=0)  81.4 us
    psum x2, blocking collectives, shards(): lax.psum(jnp.sum(projected * precond, axis=(0, 2)), ('sub', 'grp'))  78.6 us
    all_gather x5, blocking collectives, gathered(): everything = lax.all_gather(grouped, 'sub', axis=1, tiled=True)  53.8 us
    psum x1, blocking collectives, shards(): curvature = lax.psum(partial_dot, ('sub', 'grp'))  40.3 us
    ppermute x12, starting transfers between devices, extended(): lax.ppermute(lax.slice_in_dim(block, block.shape[dim] - width, None, axis...  37.6 us
    ppermute x12, waiting for transfers between devices, extended(): lax.ppermute(lax.slice_in_dim(block, 0, width, axis=dim), axis, backward)  22.3 us
    ppermute x10, starting transfers between devices, gathered(): lax.ppermute(line, 'grp', [(d, (d - have) % ways) for d in range(ways)])  19.3 us
  transfers between devices with their start and end apart: 34, of which 15 were waited for; matrix products, arithmetic and copies ran while one was open for 35% of the time, Pallas kernels for 0%

profile of v1, /device:TPU:0, one launch (start us, length us, event | category | flops | bytes accessed | tf_op | source)
XLA Modules:
  0.0 610.2 jit_solution(16079366385901529966)
XLA Ops:
  2.9 8.0 %scatter_custom_fusion = s32[2048]{0:T(1024)S(1)} fusion(s32[2048]{0:T(1024)S(1)} %bitcast.416, s32[2048]{0:T(1024)S(1)} %bitcast.415, s32[]{:T(128)} %constant.41.clone.1), kind=kCustom, calls=%fused_computation.244 | custom fusion | bytes 8196
  13.8 13.0 %gather_fusion.1 = f32[2048,96]{1,0:T(8,128)S(1)} fusion(f32[2,96,1024]{1,2,0:T(8,128)S(1)} %bitcast.386, s32[2048]{0:T(1024)S(1)} %bitcast.385), kind=kCustom, calls=%fused_computation.clone | custom fusion | bytes 1589248 | tf_op jit(solution)/shard_map/jit(take_along_axis)/gather | solution.py:62
  28.6 2.4 collective-permute-start
  33.3 5.0 collective-permute-start.2
  40.1 13.0 %gather_fusion = f32[2048,6]{1,0:T(8,128)S(1)} fusion(f32[2,6,1024]{1,2,0:T(8,128)S(1)} %bitcast.401, s32[2048]{0:T(1024)S(1)} %get-tuple-element.64), kind=kCustom, calls=%fused_computation.7 | custom fusion | bytes 114688 | tf_op jit(solution)/shard_map/jit(take_along_axis)/gather | solution.py:80
  53.6 4.0 collective-permute-start.6
  60.0 3.3 collective-permute-done.7
  63.3 5.2 collective-permute-start.8
  75.1 4.7 collective-permute-start.4
  82.8 3.1 collective-permute-done.5
  85.9 12.6 %all_gather.15 = f32[4,16,6,96]{3,2,1,0:T(8,128)S(1)} all-gather(f32[4,2,6,96]{3,2,1,0:T(8,128)S(1)} %fusion.76), channel_id=1, replica_groups=mesh['sub'=8,'grp'=4] {'sub'}, dimensions={1}, use_global_device_ids=true | all-gather | bytes 165888 | tf_op jit(solution)/shard_map/all_gather | solution.py:117
  101.7 4.1 collective-permute-start.10
  105.8 42.1 %gather_fusion.4 = bf16[2048,1024]{1,0:T(8,128)(2,1)} fusion(bf16[2,1024,1024]{2,1,0:T(8,128)(2,1)} %bitcast.383, s32[2048]{0:T(1024)S(1)} %get-tuple-element.63), kind=kCustom, calls=%fused_computation.5.clone | custom fusion | bytes 8404992 | tf_op jit(solution)/shard_map/vmap(jit(_take))/gather | solution.py:34
  148.0 6.2 %copy.88 = bf16[2,1024,1024]{1,2,0:T(8,128)(2,1)} copy(bf16[2,1024,1024]{2,1,0:T(8,128)(2,1)} %bitcast.387) | data formatting | bytes 8388608 | tf_op jit(solution)/shard_map/vmap(jit(_take))/gather | solution.py:34
  154.1 42.1 %gather_fusion.2 = bf16[2048,1024]{1,0:T(8,128)(2,1)} fusion(bf16[2,1024,1024]{2,1,0:T(8,128)(2,1)} %bitcast.384, s32[2048]{0:T(1024)S(1)} %get-tuple-element.63), kind=kCustom, calls=%fused_computation.1.clone | custom fusion | bytes 8404992 | tf_op jit(solution)/shard_map/vmap(jit(_take))/gather | solution.py:34
  196.3 6.3 %copy.80 = bf16[2,1024,1024]{1,2,0:T(8,128)(2,1)} copy(bf16[2,1024,1024]{2,1,0:T(8,128)(2,1)} %bitcast.388) | data formatting | bytes 8388608 | tf_op jit(solution)/shard_map/vmap(jit(_take))/gather | solution.py:34
  202.6 7.4 %select_bitcast_fusion = (bf16[2,1024,1024]{2,1,0:T(8,128)(2,1)}, bf16[2,1024,1024]{2,1,0:T(8,128)(2,1)}) fusion(bf16[2,1024,1024]{1,2,0:T(8,128)(2,1)} %copy.88, pred[2,1024]{1,0:T(4,128)(4,1)S(1)} %copy-done.15, bf16[2,1024,1024]{1,2,0:T(8,128)(2,1)} %copy.80), kind=kLoop, calls=%fused_computation.9 | loop fusion | flops 4194304 | bytes 16779264 | tf_op jit(solution)/shard_map/vmap()/transpose | solution.py:35
  210.1 40.8 %gather_fusion.3 = bf16[2048,1024]{1,0:T(8,128)(2,1)} fusion(bf16[2,1024,1024]{2,1,0:T(8,128)(2,1)} %get-tuple-element.58, s32[2048]{0:T(1024)S(1)} %get-tuple-element.63), kind=kCustom, calls=%fused_computation.4.clone | custom fusion | bytes 8404992 | tf_op jit(solution)/shard_map/vmap(jit(_take))/gather | solution.py:36
  250.9 8.2 %all_gather.16 = f32[4,16,6,96]{3,2,1,0:T(8,128)S(1)} all-gather(f32[4,2,6,96]{3,2,1,0:T(8,128)S(1)} %fusion.71), channel_id=1, replica_groups=mesh['sub'=8,'grp'=4] {'sub'}, dimensions={1}, use_global_device_ids=true | all-gather | bytes 165888 | tf_op jit(solution)/shard_map/all_gather | solution.py:117
  268.2 2.4 collective-permute-start.14
  274.6 5.1 collective-permute-done.15
  284.0 3.5 collective-permute-done.16
  288.7 40.6 %gather_fusion.5 = bf16[2048,1024]{1,0:T(8,128)(2,1)} fusion(bf16[2,1024,1024]{2,1,0:T(8,128)(2,1)} %get-tuple-element.57, s32[2048]{0:T(1024)S(1)} %get-tuple-element.63), kind=kCustom, calls=%fused_computation.6.clone | custom fusion | bytes 8404992 | tf_op jit(solution)/shard_map/vmap(jit(_take))/gather | solution.py:36
  329.4 12.2 %all_gather.17 = f32[4,16,6,96]{3,2,1,0:T(8,128)S(1)} all-gather(f32[4,2,6,96]{3,2,1,0:T(8,128)S(1)} %fusion.66), channel_id=1, replica_groups=mesh['sub'=8,'grp'=4] {'sub'}, dimensions={1}, use_global_device_ids=true | all-gather | bytes 165888 | tf_op jit(solution)/shard_map/all_gather | solution.py:117
  346.8 2.3 collective-permute-start.18
  350.8 3.4 collective-permute-start.20
  356.3 3.0 collective-permute-done.20
  359.3 4.4 collective-permute-done.21
  367.1 39.1 %all-reduce = (f32[96]{0:T(128)S(1)}, f32[96]{0:T(128)S(1)}) all-reduce(f32[96]{0:T(128)S(1)} %copy-done.19, f32[96]{0:T(128)S(1)} %get-tuple-element.11), channel_id=1, replica_groups=mesh['sub'=8,'grp'=4] {'sub','grp'}, use_global_device_ids=true, to_apply=%region_1.5 | all-reduce | flops 192 | bytes 1536 | tf_op jit(solution)/shard_map/psum | solution.py:142
  407.1 2.3 collective-permute-start.22
  411.6 3.8 collective-permute-done.23
  415.5 10.5 %all_gather.18 = f32[4,16,6,96]{3,2,1,0:T(8,128)S(1)} all-gather(f32[4,2,6,96]{3,2,1,0:T(8,128)S(1)} %fusion.61), channel_id=1, replica_groups=mesh['sub'=8,'grp'=4] {'sub'}, dimensions={1}, use_global_device_ids=true | all-gather | bytes 165888 | tf_op jit(solution)/shard_map/all_gather | solution.py:117
  431.8 2.3 collective-permute-start.24
  435.7 3.6 collective-permute-start.26
  441.5 2.5 collective-permute-done.26
  444.0 4.7 collective-permute-done.27
  457.1 2.9 collective-permute-start.29
  460.0 39.5 %psum.30 = f32[96]{0:T(128)S(1)} all-reduce(f32[96]{0:T(128)S(1)} %get-tuple-element.9), channel_id=1, replica_groups=mesh['sub'=8,'grp'=4] {'sub','grp'}, use_global_device_ids=true, to_apply=%region_5.9 | all-reduce | flops 96 | bytes 768 | tf_op jit(solution)/shard_map/psum | solution.py:142
  499.6 10.3 %all_gather.19 = f32[4,16,6,96]{3,2,1,0:T(8,128)S(1)} all-gather(f32[4,2,6,96]{3,2,1,0:T(8,128)S(1)} %fusion.56), channel_id=1, replica_groups=mesh['sub'=8,'grp'=4] {'sub'}, dimensions={1}, use_global_device_ids=true | all-gather | bytes 165888 | tf_op jit(solution)/shard_map/all_gather | solution.py:117
  512.7 2.5 fusion.2
  517.0 2.3 collective-permute-start.30
  520.9 2.6 collective-permute-start.32
  527.3 4.7 collective-permute-done.33
  534.0 2.5 multiply_reduce_fusion
  536.6 40.3 %psum.31 = f32[96]{0:T(128)S(1)} all-reduce(f32[96]{0:T(128)S(1)} %get-tuple-element.7), channel_id=1, replica_groups=mesh['sub'=8,'grp'=4] {'sub','grp'}, use_global_device_ids=true, to_apply=%region_7.11 | all-reduce | flops 96 | bytes 768 | tf_op jit(solution)/shard_map/psum | solution.py:149
  576.9 2.3 multiply_subtract_fusion
  580.7 13.0 %gather_fusion.7 = f32[2048,96]{1,0:T(8,128)S(1)} fusion(f32[2,96,1024]{1,2,0:T(8,128)S(1)} %copy.109, s32[2048]{0:T(1024)S(1)} %bitcast.381), kind=kCustom, calls=%fused_computation.3.clone | custom fusion | bytes 1589248 | tf_op jit(solution)/shard_map/jit(take_along_axis)/gather | solution.py:155
  595.3 13.0 %gather_fusion.6 = f32[2048,96]{1,0:T(8,128)S(1)} fusion(f32[2,96,1024]{1,2,0:T(8,128)S(1)} %copy.107, s32[2048]{0:T(1024)S(1)} %bitcast.382), kind=kCustom, calls=%fused_computation.2.clone | custom fusion | bytes 1589248 | tf_op jit(solution)/shard_map/jit(take_along_axis)/gather | solution.py:154
  (248 shorter events, 94.7 us)
Async XLA Ops:
  26.8 12.8 %copy-start.9 = (s32[1,2,1024]{2,1,0:T(2,128)S(1)}, s32[1,2,1024]{2,1,0:T(2,128)}, u32[]{:S(2)}) copy-start(s32[1,2,1024]{2,1,0:T(2,128)} %param.17) | copy-start | bytes 24580
  26.8 12.8 %copy-start.12 = (f32[1,2,6,384]{3,1,2,0:T(2,128)S(1)}, f32[1,2,6,384]{3,1,2,0:T(2,128)}, u32[]{:S(2)}) copy-start(f32[1,2,6,384]{3,1,2,0:T(2,128)} %param.16) | copy-start | bytes 55300
  26.8 12.8 %copy-start.13 = (f32[1,2,6,1024]{3,1,2,0:T(2,128)S(1)}, f32[1,2,6,1024]{3,1,2,0:T(2,128)}, u32[]{:S(2)}) copy-start(f32[1,2,6,1024]{3,1,2,0:T(2,128)} %param.15) | copy-start | bytes 147460
  28.6 40.5 %collective-permute-start = (f32[1,96,256]{2,0,1:T(1,128)S(1)}, f32[1,96,256]{2,0,1:T(1,128)S(1)}, u32[]{:S(2)}, u32[]{:S(2)}) collective-permute-start(f32[1,96,256]{2,0,1:T(1,128)S(1)} %get-tuple-element.39), channel_id=1, source_target_pairs={{0,4},{4,8},{8,12},{12,16},{16,20},{20,24},{24,28},{1,5},{5,9},{9,... | collective-permute-start | bytes 294920 | tf_op jit(solution)/shard_map/ppermute | solution.py:16
  31.0 39.8 %collective-permute-start.1 = (f32[1,96,256]{2,0,1:T(1,128)}, f32[1,96,256]{2,0,1:T(1,128)}, u32[]{:S(2)}, u32[]{:S(2)}) collective-permute-start(f32[1,96,256]{2,0,1:T(1,128)} %get-tuple-element.40), channel_id=1, source_target_pairs={{4,0},{8,4},{12,8},{16,12},{20,16},{24,20},{28,24},{5,1},{9,5},{13... | collective-permute-start | bytes 294920 | tf_op jit(solution)/shard_map/ppermute | solution.py:19
  33.3 38.7 %collective-permute-start.2 = (f32[1,2,96,256]{3,0,2,1:T(1,128)}, f32[1,2,96,256]{3,0,2,1:T(1,128)}, u32[]{:S(2)}, u32[]{:S(2)}) collective-permute-start(f32[1,2,96,256]{3,0,2,1:T(1,128)} %get-tuple-element.43), channel_id=1, source_target_pairs={{0,1},{1,2},{2,3},{4,5},{5,6},{6,7},{8,9},{9,10},{10,11},{12,13},{... | collective-permute-start | bytes 589832 | tf_op jit(solution)/shard_map/ppermute | solution.py:16
  38.3 33.7 %collective-permute-start.3 = (f32[1,2,96,256]{3,0,2,1:T(1,128)}, f32[1,2,96,256]{3,0,2,1:T(1,128)}, u32[]{:S(2)}, u32[]{:S(2)}) collective-permute-start(f32[1,2,96,256]{3,0,2,1:T(1,128)} %get-tuple-element.44), channel_id=1, source_target_pairs={{1,0},{2,1},{3,2},{5,4},{6,5},{7,6},{9,8},{10,9},{11,10},{13,12},{... | collective-permute-start | bytes 589832 | tf_op jit(solution)/shard_map/ppermute | solution.py:19
  53.6 5.1 collective-permute-start.6
  57.7 17.5 %copy-start.14 = (pred[2,1024]{1,0:T(4,128)(4,1)}, pred[2,1024]{1,0:T(4,128)(4,1)S(1)}, u32[]{:S(2)}) copy-start(pred[2,1024]{1,0:T(4,128)(4,1)S(1)} %compare_and_fusion.1) | copy-start | bytes 6148
  58.7 4.6 collective-permute-start.7
  63.3 16.5 %collective-permute-start.8 = (f32[1,2,6,640]{3,2,1,0:T(8,128)}, f32[1,2,6,640]{3,2,1,0:T(8,128)}, u32[]{:S(2)}, u32[]{:S(2)}) collective-permute-start(f32[1,2,6,640]{3,2,1,0:T(8,128)} %get-tuple-element.49), channel_id=1, source_target_pairs={{0,1},{1,2},{2,3},{4,5},{5,6},{6,7},{8,9},{9,10},{10,11},{12,13},{... | collective-permute-start | bytes 92168 | tf_op jit(solution)/shard_map/ppermute | solution.py:16
  69.1 10.7 %collective-permute-start.9 = (f32[1,2,6,640]{3,2,1,0:T(8,128)}, f32[1,2,6,640]{3,2,1,0:T(8,128)}, u32[]{:S(2)}, u32[]{:S(2)}) collective-permute-start(f32[1,2,6,640]{3,2,1,0:T(8,128)} %get-tuple-element.50), channel_id=1, source_target_pairs={{1,0},{2,1},{3,2},{5,4},{6,5},{7,6},{9,8},{10,9},{11,10},{13,12},{... | collective-permute-start | bytes 92168 | tf_op jit(solution)/shard_map/ppermute | solution.py:19
  73.8 6.0 copy-start.8
  75.1 6.0 collective-permute-start.4
  81.2 4.6 collective-permute-start.5
  101.7 100.8 %collective-permute-start.10 = (f32[1,2,6,96]{3,2,1,0:T(8,128)S(1)}, f32[1,2,6,96]{3,2,1,0:T(8,128)S(1)}, u32[]{:S(2)}, u32[]{:S(2)}) collective-permute-start(f32[1,2,6,96]{3,2,1,0:T(8,128)S(1)} %convolution_bitcast_fusion.12), channel_id=1, source_target_pairs={{0,3},{1,0},{2,1},{3,2},{4,7},{5,4},{6,5},{7,6},{8,11},{9,8},{10,9... | collective-permute-start | bytes 13832 | tf_op jit(solution)/shard_map/ppermute | solution.py:112
  196.3 6.3 %copy-start.15 = (pred[2,1024]{1,0:T(4,128)(4,1)S(1)}, pred[2,1024]{1,0:T(4,128)(4,1)}, u32[]{:S(2)}) copy-start(pred[2,1024]{1,0:T(4,128)(4,1)} %copy-done.14) | copy-start | bytes 6148
  202.6 48.3 %collective-permute-start.11 = (f32[2,2,6,96]{3,2,1,0:T(8,128)S(1)}, f32[2,2,6,96]{3,2,1,0:T(8,128)S(1)}, u32[]{:S(2)}, u32[]{:S(2)}) collective-permute-start(f32[2,2,6,96]{3,2,1,0:T(8,128)S(1)} %pad_maximum_fusion.9), channel_id=1, source_target_pairs={{0,2},{1,3},{2,0},{3,1},{4,6},{5,7},{6,4},{7,5},{8,10},{9,11},{10,... | collective-permute-start | bytes 27656 | tf_op jit(solution)/shard_map/ppermute | solution.py:112
  264.3 7.7 %collective-permute-start.12 = (f32[1,96,256]{2,0,1:T(1,128)S(1)}, f32[1,96,256]{2,0,1:T(1,128)S(1)}, u32[]{:S(2)}, u32[]{:S(2)}) collective-permute-start(f32[1,96,256]{2,0,1:T(1,128)S(1)} %get-tuple-element.33), channel_id=1, source_target_pairs={{0,4},{4,8},{8,12},{12,16},{16,20},{20,24},{24,28},{1,5},{5,9},{9,... | collective-permute-start | bytes 294920 | tf_op jit(solution)/shard_map/ppermute | solution.py:16
  266.9 5.5 collective-permute-start.13
  268.2 6.4 %collective-permute-start.14 = (f32[1,2,96,256]{3,0,2,1:T(1,128)S(1)}, f32[1,2,96,256]{3,0,2,1:T(1,128)S(1)}, u32[]{:S(2)}, u32[]{:S(2)}) collective-permute-start(f32[1,2,96,256]{3,0,2,1:T(1,128)S(1)} %get-tuple-element.37), channel_id=1, source_target_pairs={{0,1},{1,2},{2,3},{4,5},{5,6},{6,7},{8,9},{9,10},{10,11},{12,13},{... | collective-permute-start | bytes 589832 | tf_op jit(solution)/shard_map/ppermute | solution.py:16
  270.6 9.1 %collective-permute-start.15 = (f32[1,2,96,256]{3,0,2,1:T(1,128)S(1)}, f32[1,2,96,256]{3,0,2,1:T(1,128)S(1)}, u32[]{:S(2)}, u32[]{:S(2)}) collective-permute-start(f32[1,2,96,256]{3,0,2,1:T(1,128)S(1)} %get-tuple-element.38), channel_id=1, source_target_pairs={{1,0},{2,1},{3,2},{5,4},{6,5},{7,6},{9,8},{10,9},{11,10},{13,12},{... | collective-permute-start | bytes 589832 | tf_op jit(solution)/shard_map/ppermute | solution.py:19
  283.5 4.0 collective-permute-start.16
  287.5 41.8 %collective-permute-start.17 = (f32[2,2,6,96]{3,2,1,0:T(8,128)S(1)}, f32[2,2,6,96]{3,2,1,0:T(8,128)S(1)}, u32[]{:S(2)}, u32[]{:S(2)}) collective-permute-start(f32[2,2,6,96]{3,2,1,0:T(8,128)S(1)} %pad_maximum_fusion.10), channel_id=1, source_target_pairs={{0,2},{1,3},{2,0},{3,1},{4,6},{5,7},{6,4},{7,5},{8,10},{9,11},{10,... | collective-permute-start | bytes 27656 | tf_op jit(solution)/shard_map/ppermute | solution.py:112
  346.8 20.3 %copy-start.19 = (f32[96]{0:T(128)S(1)}, f32[96]{0:T(128)}, u32[]{:S(2)}) copy-start(f32[96]{0:T(128)} %get-tuple-element.13) | copy-start | bytes 1156
  346.8 8.6 %collective-permute-start.18 = (f32[1,96,256]{2,0,1:T(1,128)S(1)}, f32[1,96,256]{2,0,1:T(1,128)S(1)}, u32[]{:S(2)}, u32[]{:S(2)}) collective-permute-start(f32[1,96,256]{2,0,1:T(1,128)S(1)} %get-tuple-element.27), channel_id=1, source_target_pairs={{0,4},{4,8},{8,12},{12,16},{16,20},{20,24},{24,28},{1,5},{5,9},{9,... | collective-permute-start | bytes 294920 | tf_op jit(solution)/shard_map/ppermute | solution.py:16
  349.5 6.4 %collective-permute-start.19 = (f32[1,96,256]{2,0,1:T(1,128)S(1)}, f32[1,96,256]{2,0,1:T(1,128)S(1)}, u32[]{:S(2)}, u32[]{:S(2)}) collective-permute-start(f32[1,96,256]{2,0,1:T(1,128)S(1)} %get-tuple-element.28), channel_id=1, source_target_pairs={{4,0},{8,4},{12,8},{16,12},{20,16},{24,20},{28,24},{5,1},{9,5},{13... | collective-permute-start | bytes 294920 | tf_op jit(solution)/shard_map/ppermute | solution.py:19
  350.8 8.5 %collective-permute-start.20 = (f32[1,2,96,256]{3,0,2,1:T(1,128)S(1)}, f32[1,2,96,256]{3,0,2,1:T(1,128)S(1)}, u32[]{:S(2)}, u32[]{:S(2)}) collective-permute-start(f32[1,2,96,256]{3,0,2,1:T(1,128)S(1)} %get-tuple-element.31), channel_id=1, source_target_pairs={{0,1},{1,2},{2,3},{4,5},{5,6},{6,7},{8,9},{9,10},{10,11},{12,13},{... | collective-permute-start | bytes 589832 | tf_op jit(solution)/shard_map/ppermute | solution.py:16
  354.2 9.5 %collective-permute-start.21 = (f32[1,2,96,256]{3,0,2,1:T(1,128)S(1)}, f32[1,2,96,256]{3,0,2,1:T(1,128)S(1)}, u32[]{:S(2)}, u32[]{:S(2)}) collective-permute-start(f32[1,2,96,256]{3,0,2,1:T(1,128)S(1)} %get-tuple-element.32), channel_id=1, source_target_pairs={{1,0},{2,1},{3,2},{5,4},{6,5},{7,6},{9,8},{10,9},{11,10},{13,12},{... | collective-permute-start | bytes 589832 | tf_op jit(solution)/shard_map/ppermute | solution.py:19
  406.2 3.2 copy-start.20
  407.1 3.7 collective-permute-start.22
  410.8 4.6 collective-permute-start.23
  431.1 18.3 %copy-start.5 = (f32[2,96,1024]{2,1,0:T(8,128)}, f32[2,96,1024]{2,1,0:T(8,128)S(1)}, u32[]{:S(2)}) copy-start(f32[2,96,1024]{2,1,0:T(8,128)S(1)} %fusion) | copy-start | bytes 2359300
  431.8 8.9 %collective-permute-start.24 = (f32[1,96,256]{2,0,1:T(1,128)S(1)}, f32[1,96,256]{2,0,1:T(1,128)S(1)}, u32[]{:S(2)}, u32[]{:S(2)}) collective-permute-start(f32[1,96,256]{2,0,1:T(1,128)S(1)} %get-tuple-element.21), channel_id=1, source_target_pairs={{0,4},{4,8},{8,12},{12,16},{16,20},{20,24},{24,28},{1,5},{5,9},{9,... | collective-permute-start | bytes 294920 | tf_op jit(solution)/shard_map/ppermute | solution.py:16
  434.4 6.7 %collective-permute-start.25 = (f32[1,96,256]{2,0,1:T(1,128)S(1)}, f32[1,96,256]{2,0,1:T(1,128)S(1)}, u32[]{:S(2)}, u32[]{:S(2)}) collective-permute-start(f32[1,96,256]{2,0,1:T(1,128)S(1)} %get-tuple-element.22), channel_id=1, source_target_pairs={{4,0},{8,4},{12,8},{16,12},{20,16},{24,20},{28,24},{5,1},{9,5},{13... | collective-permute-start | bytes 294920 | tf_op jit(solution)/shard_map/ppermute | solution.py:19
  435.7 8.2 %collective-permute-start.26 = (f32[1,2,96,256]{3,0,2,1:T(1,128)S(1)}, f32[1,2,96,256]{3,0,2,1:T(1,128)S(1)}, u32[]{:S(2)}, u32[]{:S(2)}) collective-permute-start(f32[1,2,96,256]{3,0,2,1:T(1,128)S(1)} %get-tuple-element.25), channel_id=1, source_target_pairs={{0,1},{1,2},{2,3},{4,5},{5,6},{6,7},{8,9},{9,10},{10,11},{12,13},{... | collective-permute-start | bytes 589832 | tf_op jit(solution)/shard_map/ppermute | solution.py:16
  439.4 9.3 %collective-permute-start.27 = (f32[1,2,96,256]{3,0,2,1:T(1,128)S(1)}, f32[1,2,96,256]{3,0,2,1:T(1,128)S(1)}, u32[]{:S(2)}, u32[]{:S(2)}) collective-permute-start(f32[1,2,96,256]{3,0,2,1:T(1,128)S(1)} %get-tuple-element.26), channel_id=1, source_target_pairs={{1,0},{2,1},{3,2},{5,4},{6,5},{7,6},{9,8},{10,9},{11,10},{13,12},{... | collective-permute-start | bytes 589832 | tf_op jit(solution)/shard_map/ppermute | solution.py:19
  440.9 19.1 %copy-start.11 = (s32[2,1,1024]{2,0,1:T(2,128)S(1)}, s32[2,1,1024]{2,0,1:T(2,128)}, u32[]{:S(2)}) copy-start(s32[2,1,1024]{2,0,1:T(2,128)} %copy-done.10) | copy-start | bytes 24580
  440.9 58.7 %copy-start.21 = (f32[96]{0:T(128)S(1)}, f32[96]{0:T(128)}, u32[]{:S(2)}) copy-start(f32[96]{0:T(128)} %copy-done.20) | copy-start | bytes 1156
  453.4 3.7 collective-permute-start.28
  457.1 42.5 %collective-permute-start.29 = (f32[2,2,6,96]{3,2,1,0:T(8,128)S(1)}, f32[2,2,6,96]{3,2,1,0:T(8,128)S(1)}, u32[]{:S(2)}, u32[]{:S(2)}) collective-permute-start(f32[2,2,6,96]{3,2,1,0:T(8,128)S(1)} %pad_maximum_fusion.12), channel_id=1, source_target_pairs={{0,2},{1,3},{2,0},{3,1},{4,6},{5,7},{6,4},{7,5},{8,10},{9,11},{10,... | collective-permute-start | bytes 27656 | tf_op jit(solution)/shard_map/ppermute | solution.py:112
  517.0 60.0 %copy-start.18 = (f32[96]{0:T(128)S(1)}, f32[96]{0:T(128)}, u32[]{:S(2)}) copy-start(f32[96]{0:T(128)} %copy-done.17) | copy-start | bytes 1156
  517.0 7.8 %collective-permute-start.30 = (f32[1,96,256]{2,0,1:T(1,128)S(1)}, f32[1,96,256]{2,0,1:T(1,128)S(1)}, u32[]{:S(2)}, u32[]{:S(2)}) collective-permute-start(f32[1,96,256]{2,0,1:T(1,128)S(1)} %get-tuple-element.15), channel_id=1, source_target_pairs={{0,4},{4,8},{8,12},{12,16},{16,20},{20,24},{24,28},{1,5},{5,9},{9,... | collective-permute-start | bytes 294920 | tf_op jit(solution)/shard_map/ppermute | solution.py:16
  519.6 5.6 collective-permute-start.31
  520.9 6.4 %collective-permute-start.32 = (f32[1,2,96,256]{3,0,2,1:T(1,128)S(1)}, f32[1,2,96,256]{3,0,2,1:T(1,128)S(1)}, u32[]{:S(2)}, u32[]{:S(2)}) collective-permute-start(f32[1,2,96,256]{3,0,2,1:T(1,128)S(1)} %get-tuple-element.19), channel_id=1, source_target_pairs={{0,1},{1,2},{2,3},{4,5},{5,6},{6,7},{8,9},{9,10},{10,11},{12,13},{... | collective-permute-start | bytes 589832 | tf_op jit(solution)/shard_map/ppermute | solution.py:16
  523.5 8.6 %collective-permute-start.33 = (f32[1,2,96,256]{3,0,2,1:T(1,128)S(1)}, f32[1,2,96,256]{3,0,2,1:T(1,128)S(1)}, u32[]{:S(2)}, u32[]{:S(2)}) collective-permute-start(f32[1,2,96,256]{3,0,2,1:T(1,128)S(1)} %get-tuple-element.20), channel_id=1, source_target_pairs={{1,0},{2,1},{3,2},{5,4},{6,5},{7,6},{9,8},{10,9},{11,10},{13,12},{... | collective-permute-start | bytes 589832 | tf_op jit(solution)/shard_map/ppermute | solution.py:19
  595.3 13.4 %copy-start.4 = (f32[2,1024,96]{1,2,0:T(8,128)S(1)}, f32[2,1024,96]{1,2,0:T(8,128)}, u32[]{:S(2)}) copy-start(f32[2,1024,96]{1,2,0:T(8,128)} %copy.110) | copy-start | bytes 2359300
  595.3 13.4 %copy-start.16 = (pred[2,1024]{1,0:T(4,128)(4,1)S(1)}, pred[2,1024]{1,0:T(4,128)(4,1)}, u32[]{:S(2)}) copy-start(pred[2,1024]{1,0:T(4,128)(4,1)} %get-tuple-element.61) | copy-start | bytes 6148
  (8 other events, 17.1 us)
